TPU v7x, 256 devices: a whole 4x4x8 slice. The times are simulated.
256 devices in a mesh: expert: 16 (over y_hi, z), mp: 8 (over y_lo, x), batch: 2 (over core).
Axes of the slice: x: 4, y: 4 (y_hi: 2, y_lo: 2; y = y_hi * 2 + y_lo), z: 8, core: 2. Of those that a mesh axis runs over, the one named last changes fastest.
Arguments:
- tokens: bfloat16 [2, 2048, 2880], P('batch', 'expert', 'mp'), may hold values from -6 to 6
- segments: int32 [2, 2048], P('batch'), may hold values from 0 to 63, never falling along the last dimension, each value on 1 to 1024 neighbouring positions
- attn_gain: float32 [2880], replicated, may hold values from 0.6 to 9
- w_query: bfloat16 [2880, 4096], P('expert', 'mp'), may hold values from -0.109375 to 0.109375
- key_weight: bfloat16 [2880, 512], P('expert', 'mp'), may hold values from -0.109375 to 0.109375
- value_weight: bfloat16 [2880, 512], P('expert', 'mp'), may hold values from -0.109375 to 0.109375
- w_out: bfloat16 [4096, 2880], P('mp', 'expert'), may hold values from -0.09375 to 0.09375
- sink_head_logit: float32 [64], P('mp'), may hold values from -4 to 4
- moe_gain: float32 [2880], replicated, may hold values from 0.5 to 1.5
- expert_in: bfloat16 [16, 2, 2880, 2880], P('expert', None, None, 'mp'), may hold values from -0.3125 to 0.3125
- expert_down: bfloat16 [16, 2880, 2880], P('expert', 'mp'), may hold values from -0.01953125 to 0.01953125
- routes: int32 [2, 2048, 4], P('batch', 'expert'), may hold values from 0 to 15, all different within a row; in each aligned block of 128 rows (0 to 127, 128 to 255, ..., all dimensions but the last counted through in order) at most 48 rows name the same one
- route_weights: float32 [2, 2048, 4], P('batch', 'expert'), may hold values from 0.1 to 1
Outputs:
- hidden: bfloat16 [2, 2048, 2880], P('batch', 'expert', 'mp')
- key_cache: bfloat16 [2, 2048, 512], P('batch', 'expert', 'mp')
- value_cache: bfloat16 [2, 2048, 512], P('batch', 'expert', 'mp')
Inputs may be any that keep to these rules, and one draw needn't show every extreme that they name: Within each aligned block of 128 tokens of a micro-batch (the tokens of one index of expert), no expert is named by more than 48 routes; a token's routes name different experts. `segments`: segment numbers never fall along a micro-batch; one segment holds at most 1024 tokens.
All inputs are finite; a program needn't handle non-finite values.
Results may differ from a plain program's by a relative error of at most 0.024.
The roundings to bfloat16 on the way count: a program that leaves them out, or rounds other values in their place, can miss the bound.
Values may be sent and summed in bfloat16 or wider, within the bound.
No kernel may reach another device: no remote copies, remote signals or barrier semaphores. Data moves between devices by JAX's collectives and lax.ppermute only.
A program may use at most 64 MiB of HBM per device.

v0:
```python
import math
import jax
import jax.numpy as jnp
from jax import lax
from jax.sharding import PartitionSpec as P

HEAD_SIZE = 64
eps = 1e-05
rope_base = 150000.0
clamp_limit = 7.0
glu_alpha = 1.702


def rms_norm(row_block, gain):
    values = row_block.astype(jnp.float32)
    inv_scale = lax.rsqrt(jnp.mean(values * values, axis=-1, keepdims=True) + eps)
    return (values * inv_scale * gain).astype(jnp.bfloat16)


def apply_rotary(values, token_positions):
    half_dim = values.shape[-1] // 2
    inv_freq = jnp.power(
        rope_base, -2.0 * jnp.arange(half_dim, dtype=jnp.float32) / values.shape[-1]
    )
    rot_angle = token_positions.astype(jnp.float32)[:, None] * inv_freq[None, :]
    cosine = jnp.cos(rot_angle)[:, None, :]
    sine_val = jnp.sin(rot_angle)[:, None, :]
    first_half = values[..., :half_dim]
    second_half = values[..., half_dim:]
    return jnp.concatenate(
        [
            first_half * cosine - second_half * sine_val,
            second_half * cosine + first_half * sine_val,
        ],
        axis=-1,
    )


def expert_rows(row_block, w_in, w_down):
    gate_val = jnp.dot(row_block, w_in[0], preferred_element_type=jnp.float32)
    up_val = jnp.dot(row_block, w_in[1], preferred_element_type=jnp.float32)
    gate_val = jnp.minimum(gate_val, clamp_limit)
    up_val = jnp.clip(up_val, -clamp_limit, clamp_limit)
    activated = ((up_val + 1.0) * gate_val * jax.nn.sigmoid(glu_alpha * gate_val)).astype(
        jnp.bfloat16
    )
    return jnp.dot(activated, w_down, preferred_element_type=jnp.float32)


def shards(
    tokens,
    segments,
    attn_gain,
    w_query,
    key_weight,
    value_weight,
    w_out,
    sink_head_logit,
    moe_gain,
    expert_in,
    expert_down,
    routes,
    route_weights,
):
    local_rows = tokens[0]
    tok_count = local_rows.shape[0]
    expert_devs = lax.axis_size("expert")
    row_start = lax.axis_index("expert") * tok_count
    whole_rows = lax.all_gather(local_rows, "mp", axis=1, tiled=True)
    input_normalised = rms_norm(whole_rows, attn_gain)
    query_cols = w_query.shape[1]
    kv_cols = key_weight.shape[1]
    weight_parts = (
        lax.all_gather(w_query, "expert", axis=0, tiled=True),
        lax.all_gather(key_weight, "expert", axis=0, tiled=True),
        lax.all_gather(value_weight, "expert", axis=0, tiled=True),
    )
    query_raw, key_raw, value_raw = tuple(
        (
            jnp.dot(input_normalised, weight_part, preferred_element_type=jnp.float32)
            for weight_part in weight_parts
        )
    )
    token_positions = row_start + jnp.arange(tok_count, dtype=jnp.int32)
    query_by_head = query_cols // HEAD_SIZE
    kv_heads = kv_cols // HEAD_SIZE
    heads_per_group = query_by_head // kv_heads
    query_matrix = apply_rotary(
        query_raw.reshape(tok_count, query_by_head, HEAD_SIZE), token_positions
    ).astype(jnp.bfloat16)
    key_rotary = (
        apply_rotary(key_raw.reshape(tok_count, kv_heads, HEAD_SIZE), token_positions)
        .astype(jnp.bfloat16)
        .reshape(tok_count, kv_cols)
    )
    value_fresh = value_raw.astype(jnp.bfloat16)
    keys_all, values_all = (
        lax.all_gather(key_rotary, "expert", axis=0, tiled=True),
        lax.all_gather(value_fresh, "expert", axis=0, tiled=True),
    )
    seq_len = keys_all.shape[0]
    seg_all = segments[0]
    seg_local = lax.dynamic_slice_in_dim(seg_all, row_start, tok_count)
    row_total = heads_per_group * tok_count
    query_rows = (
        query_matrix.reshape(tok_count, kv_heads, heads_per_group, HEAD_SIZE)
        .transpose(1, 2, 0, 3)
        .reshape(kv_heads, row_total, HEAD_SIZE)
    )
    key_by_head = keys_all.reshape(seq_len, kv_heads, HEAD_SIZE).transpose(1, 0, 2)
    value_by_head = values_all.reshape(seq_len, kv_heads, HEAD_SIZE).transpose(1, 0, 2)
    row_pos = jnp.tile(token_positions, heads_per_group)
    row_seg = jnp.tile(seg_local, heads_per_group)
    sink_rows = jnp.repeat(sink_head_logit.reshape(kv_heads, heads_per_group), tok_count, axis=1)
    key_block = math.gcd(seq_len, 512)
    block_count = seq_len // key_block
    score_scale = HEAD_SIZE ** (-0.5)

    def block_scores(index):
        key_first = index * key_block
        key_part = lax.dynamic_slice_in_dim(key_by_head, key_first, key_block, 1)
        scores = (
            jnp.einsum("hrd,hkd->hrk", query_rows, key_part, preferred_element_type=jnp.float32)
            * score_scale
        )
        key_pos = key_first + jnp.arange(key_block, dtype=jnp.int32)
        key_seg = lax.dynamic_slice_in_dim(seg_all, key_first, key_block, 0)
        allowed = (key_pos[None, :] <= row_pos[:, None]) & (key_seg[None, :] == row_seg[:, None])
        return jnp.where(allowed[None], scores, -jnp.inf)

    def max_step(index, running):
        return jnp.maximum(running, jnp.max(block_scores(index), axis=-1))

    row_max = lax.fori_loop(0, block_count, max_step, sink_rows)

    def sum_step(index, carried):
        weighted, denom = carried
        probs = jnp.exp(block_scores(index) - row_max[..., None]).astype(jnp.bfloat16)
        value_part = lax.dynamic_slice_in_dim(value_by_head, index * key_block, key_block, 1)
        weighted = weighted + jnp.einsum(
            "hrk,hkd->hrd", probs, value_part, preferred_element_type=jnp.float32
        )
        denom = denom + jnp.sum(probs, axis=-1, dtype=jnp.float32)
        return (weighted, denom)

    init_pair = (
        jnp.zeros((kv_heads, row_total, HEAD_SIZE), jnp.float32),
        jnp.zeros((kv_heads, row_total), jnp.float32),
    )
    weighted, denom = lax.fori_loop(0, block_count, sum_step, init_pair)
    denom = denom + jnp.exp(sink_rows - row_max)
    mixed = (weighted / denom[..., None]).astype(jnp.bfloat16)
    mixed = (
        mixed.reshape(kv_heads, heads_per_group, tok_count, HEAD_SIZE)
        .transpose(2, 0, 1, 3)
        .reshape(tok_count, query_cols)
    )
    out_terms = jnp.dot(
        mixed,
        lax.all_gather(w_out, "expert", axis=1, tiled=True),
        preferred_element_type=jnp.float32,
    )
    attn_part = lax.psum_scatter(
        out_terms.astype(jnp.bfloat16), "mp", scatter_dimension=1, tiled=True
    ).astype(jnp.float32)
    first_out = (local_rows.astype(jnp.float32) + attn_part).astype(jnp.bfloat16)
    top_count = routes.shape[2]
    local_experts = expert_in.shape[0]
    expert_count = local_experts * expert_devs
    capacity = 3 * tok_count * top_count // (2 * expert_count)
    chosen = routes[0].reshape(tok_count * top_count)
    onehot = (chosen[:, None] == jnp.arange(expert_count, dtype=jnp.int32)[None, :]).astype(
        jnp.int32
    )
    ranks = jnp.sum((jnp.cumsum(onehot, axis=0) - onehot) * onehot, axis=1)
    target = chosen * capacity + ranks
    source_row = (
        jnp.full((expert_count * capacity,), tok_count, jnp.int32)
        .at[target]
        .set(jnp.arange(tok_count * top_count, dtype=jnp.int32) // top_count)
    )
    moe_whole = lax.all_gather(first_out, "mp", axis=1, tiled=True)
    moe_normed = rms_norm(moe_whole, moe_gain)
    padded = jnp.concatenate(
        [moe_normed, jnp.zeros((1, moe_normed.shape[1]), jnp.bfloat16)], axis=0
    )
    outgoing = padded[source_row].reshape(expert_count, capacity, padded.shape[1])
    arrived = lax.all_to_all(outgoing, "expert", split_axis=0, concat_axis=0, tiled=True)
    model_width = arrived.shape[2]
    grouped = arrived.reshape(expert_devs, local_experts, capacity, model_width)
    inputs = grouped[:, 0].reshape(expert_devs * capacity, model_width)
    partial_list = [
        expert_rows(inputs, expert_in[0], expert_down[0]).reshape(
            expert_devs, capacity, model_width
        )
    ]
    partials = jnp.stack(partial_list, axis=1).reshape(expert_count, capacity, model_width)
    expert_out = lax.psum_scatter(
        partials.astype(jnp.bfloat16), "mp", scatter_dimension=2, tiled=True
    )
    returned = lax.all_to_all(expert_out, "expert", split_axis=0, concat_axis=0, tiled=True)
    local_width = returned.shape[2]
    picked = returned.reshape(expert_count * capacity, local_width)[target].reshape(
        tok_count, top_count, local_width
    )
    moe_sum = jnp.sum(picked.astype(jnp.float32) * route_weights[0][..., None], axis=1)
    hidden = (first_out.astype(jnp.float32) + moe_sum).astype(jnp.bfloat16)
    return (hidden[None], key_rotary[None], value_fresh[None])


def solution(mesh):
    placed = (
        P("batch", "expert", "mp"),
        P("batch", None),
        P(),
        P("expert", "mp"),
        P("expert", "mp"),
        P("expert", "mp"),
        P("mp", "expert"),
        P("mp"),
        P(),
        P("expert", None, None, "mp"),
        P("expert", "mp", None),
        P("batch", "expert", None),
        P("batch", "expert", None),
    )
    return jax.shard_map(
        shards,
        mesh=mesh,
        in_specs=placed,
        out_specs=(
            P("batch", "expert", "mp"),
            P("batch", "expert", "mp"),
            P("batch", "expert", "mp"),
        ),
        check_vma=False,
    )
```

profile of v0, /device:TPU:1, one launch (start us, length us, event | category | flops | bytes accessed | tf_op | source)
XLA Modules:
  0.0 570.1 jit_solution(6893705568752840482)
XLA Ops:
  8.8 25.6 %all-gather = bf16[1,128,2880]{1,2,0:T(8,128)(2,1)S(1)} all-gather(bf16[1,128,360]{1,2,0:T(8,128)(2,1)} %param.17), channel_id=2, replica_groups=mesh['expert'=16,'mp'=8,'batch'=2] {'mp'}, dimensions={2}, use_global_device_ids=true | all-gather | bytes 829440 | tf_op jit(solution)/shard_map/all_gather | solution.py:69
  34.8 40.1 %all-gather.1 = bf16[16,180,64]{1,2,0:T(8,128)(2,1)S(1)} all-gather(bf16[1,180,64]{1,2,0:T(8,128)(2,1)} %bitcast.211), channel_id=1, replica_groups=mesh['expert'=16,'mp'=8,'batch'=2] {'expert'}, dimensions={0}, use_global_device_ids=true | all-gather | bytes 391680 | tf_op jit(solution)/shard_map/all_gather | solution.py:75
  79.3 31.8 %all_gather.26 = bf16[2048,64]{0,1:T(8,128)(2,1)S(1)} all-gather(bf16[128,64]{0,1:T(8,128)(2,1)S(1)} %pad_maximum_fusion), channel_id=1, replica_groups=mesh['expert'=16,'mp'=8,'batch'=2] {'expert'}, dimensions={0}, use_global_device_ids=true | all-gather | bytes 278528 | tf_op jit(solution)/shard_map/all_gather | solution.py:98
  112.2 33.1 %all-gather.3 = bf16[16,180,64]{1,2,0:T(8,128)(2,1)S(1)} all-gather(bf16[1,180,64]{1,2,0:T(8,128)(2,1)} %bitcast.212), channel_id=1, replica_groups=mesh['expert'=16,'mp'=8,'batch'=2] {'expert'}, dimensions={0}, use_global_device_ids=true | all-gather | bytes 391680 | tf_op jit(solution)/shard_map/all_gather | solution.py:76
  149.5 35.5 %all_gather.29 = bf16[2048,64]{0,1:T(8,128)(2,1)} all-gather(bf16[128,64]{0,1:T(8,128)(2,1)S(1)} %convolution_convert_fusion.2), channel_id=1, replica_groups=mesh['expert'=16,'mp'=8,'batch'=2] {'expert'}, dimensions={0}, use_global_device_ids=true | all-gather | bytes 278528 | tf_op jit(solution)/shard_map/all_gather | solution.py:99
  185.1 4.4 reshape.398
  189.5 3.5 fusion.80
  194.0 7.0 %while.30 = (s32[]{:T(128)}, f32[1,1024]{1,0:T(1,128)S(1)}, s32[2048]{0:T(1024)S(1)}, bf16[1,2048,64]{2,1,0:T(8,128)(2,1)}, bf16[1,1024,64]{2,1,0:T(8,128)(2,1)}...) while((s32[]{:T(128)}, f32[1,1024]{1,0:T(1,128)S(1)}, ...), condition=%wide.region_3.4_spmd.clone, body=%wide.region_1.3_spmd.clone.sunk | while | flops 70255112 | bytes 437415 | solution.py:134
  201.0 12.7 %while.31 = (s32[]{:T(128)}, f32[1,1024,64]{1,2,0:T(8,128)S(1)}, f32[1,1024]{1,0:T(1,128)S(1)}, s32[2048]{0:T(1024)S(1)}, bf16[1,2048,64]{2,1,0:T(8,128)(2,1)}, ...) while((s32[]{:T(128)}, f32[1,1024,64]{1,2,0:T(8,128)S(1)}, ...), condition=%wide.region_6.7_spmd.clone, body=%wide.region_4.6_spmd.clone.sunk | while | flops 139068928 | bytes 3128526 | solution.py:150
  213.8 4.3 reshape.402
  218.1 3.7 convolution_convert_fusion.1
  226.6 58.4 %reduce-scatter.10.cloned.1.call-done = bf16[128,360]{0,1:T(8,128)(2,1)} async-done(((bf16[128,2880]{0,1:T(8,128)(2,1)}), bf16[128,360]{0,1:T(8,128)(2,1)}) %reduce-scatter.10.cloned.1.call-update) | async-done | bytes 92176
  286.3 26.1 %all_gather.31 = bf16[128,2880]{0,1:T(8,128)(2,1)} all-gather(bf16[128,360]{0,1:T(8,128)(2,1)S(1)} %copy.84), channel_id=1, replica_groups=mesh['expert'=16,'mp'=8,'batch'=2] {'mp'}, dimensions={1}, use_global_device_ids=true | all-gather | bytes 829440 | tf_op jit(solution)/shard_map/all_gather | solution.py:182
  314.4 4.8 gather_fusion
  319.2 100.2 %all_to_all.10 = bf16[16,48,2880]{2,1,0:T(8,128)(2,1)S(1)} all-to-all(bf16[16,48,2880]{2,1,0:T(8,128)(2,1)} %bitcast.189), channel_id=1, replica_groups=mesh['expert'=16,'mp'=8,'batch'=2] {'expert'}, dimensions={0} | all-to-all | bytes 8847360 | tf_op jit(solution)/shard_map/all_to_all | solution.py:188
  419.4 3.5 fusion.38
  425.3 4.1 convolution_convert_fusion
  429.5 14.6 %copy.94 = bf16[16,48,2880]{1,0,2:T(8,128)(2,1)} copy(bf16[16,48,2880]{2,1,0:T(8,128)(2,1)} %convolution_convert_fusion) | data formatting | bytes 8847360
  444.1 17.1 %reshape.409 = bf16[2880,768]{1,0:T(8,128)(2,1)} reshape(bf16[2880,16,48]{2,1,0:T(8,128)(2,1)} %bitcast.187) | data formatting | bytes 8847360
  461.2 64.7 %reduce-scatter.8.cloned.1.call-done = bf16[360,768]{1,0:T(8,128)(2,1)} async-done(((bf16[2880,768]{1,0:T(8,128)(2,1)}), bf16[360,768]{1,0:T(8,128)(2,1)}) %reduce-scatter.8.cloned.1.call-update) | async-done | bytes 552976
  525.9 3.6 reshape.410
  529.5 2.6 copy.95
  532.1 9.0 %all-to-all-start.1 = ((bf16[16,48,360]{2,1,0:T(8,128)(2,1)}), bf16[16,48,360]{2,1,0:T(8,128)(2,1)S(1)}, u32[]{:S(2)}, u32[]{:S(2)}) async-start(bf16[16,48,360]{2,1,0:T(8,128)(2,1)} %copy.95), calls=%async_computation.1 | async-start | bytes 1179648 | tf_op jit(solution)/shard_map/all_to_all | solution.py:201
  541.8 16.6 %all-to-all-done.1 = bf16[16,48,360]{2,1,0:T(8,128)(2,1)S(1)} async-done(((bf16[16,48,360]{2,1,0:T(8,128)(2,1)}), bf16[16,48,360]{2,1,0:T(8,128)(2,1)S(1)}, u32[]{:S(2)}, u32[]{:S(2)}) %all-to-all-start.1) | async-done | bytes 552992 | tf_op jit(solution)/shard_map/all_to_all | solution.py:201
  (150 shorter events, 48.1 us)
Async XLA Ops:
  7.2 418.2 %copy-start = (bf16[1,360,2880]{2,1,0:T(8,128)(2,1)S(1)}, bf16[1,360,2880]{2,1,0:T(8,128)(2,1)}, u32[]{:S(2)}) copy-start(bf16[1,360,2880]{2,1,0:T(8,128)(2,1)} %param.27) | copy-start | bytes 6220804
  7.2 177.9 %all-gather.8.cloned.1.call-start = ((), (), s32[]{:S(2)}) async-start(), calls=%async_computation.4 | async-start | bytes 3203072 | tf_op jit(solution)/shard_map/all_gather | solution.py:74
  7.9 205.9 %all-gather.10.cloned.1.call-start = ((), (), s32[]{:S(2)}) async-start(), calls=%async_computation.5 | async-start | bytes 3203072 | tf_op jit(solution)/shard_map/all_gather | solution.py:160
  8.7 69.9 %copy-start.10 = (f32[2880]{0:T(1024)S(1)}, f32[2880]{0:T(1024)}, u32[]{:S(2)}) copy-start(f32[2880]{0:T(1024)} %param.19) | copy-start | bytes 34564
  8.7 276.4 %reduce-scatter.10.cloned.1.call-start = ((), (), s32[]{:S(2)}) async-start(), calls=%async_computation.7 | async-start | bytes 829440
  34.8 43.7 %copy-start.12 = (f32[128]{0:T(128)}, f32[128]{0:T(128)S(1)}, u32[]{:S(2)}) copy-start(f32[128]{0:T(128)S(1)} %add_rsqrt_fusion.1) | copy-start | bytes 1540
  74.9 37.3 %copy-start.9 = (f32[8]{0:T(128)S(1)}, f32[8]{0:T(128)}, u32[]{:S(2)}) copy-start(f32[8]{0:T(128)} %param.24) | copy-start | bytes 100
  112.2 72.8 %copy-start.4 = (s32[1,2048]{1,0:T(1,128)S(1)}, s32[1,2048]{1,0:T(1,128)}, u32[]{:S(2)}) copy-start(s32[1,2048]{1,0:T(1,128)} %param.18) | copy-start | bytes 24580
  149.5 35.6 %copy-start.5 = (bf16[128,64]{0,1:T(8,128)(2,1)}, bf16[128,64]{0,1:T(8,128)(2,1)S(1)}, u32[]{:S(2)}) copy-start(bf16[128,64]{0,1:T(8,128)(2,1)S(1)} %convolution_convert_fusion.2) | copy-start | bytes 49156
  185.0 4.5 copy-start.11
  185.1 4.5 copy-start.13
  189.5 3.5 copy-start.2
  189.5 3.5 copy-start.3
  218.1 3.8 copy-start.1
  218.1 3.9 copy-start.7
  221.8 304.0 %reduce-scatter.8.cloned.1.call-start = ((), (), s32[]{:S(2)}) async-start(), calls=%async_computation.6 | async-start | bytes 4976640
  222.3 91.8 %copy-start.6 = (f32[2880]{0:T(1024)S(1)}, f32[2880]{0:T(1024)}, u32[]{:S(2)}) copy-start(f32[2880]{0:T(1024)} %param.25) | copy-start | bytes 34564
  319.2 103.7 %slice-start = ((s8[4239360]{0:T(1024)(128)(4,1)}), s8[4194304]{0:T(1024)(128)(4,1)S(1)}, s32[]{:S(2)}) async-start(s8[4239360]{0:T(1024)(128)(4,1)} %bitcast.219), calls=%async_computation.8 | async-start | bytes 8388608
  419.4 3.6 slice-start.1
  529.5 11.6 %copy-start.8 = (f32[1,128,4]{1,2,0:T(4,128)S(1)}, f32[1,128,4]{1,2,0:T(4,128)}, u32[]{:S(2)}) copy-start(f32[1,128,4]{1,2,0:T(4,128)} %param.29) | copy-start | bytes 6148
  532.1 26.4 %all-to-all-start.1 = ((bf16[16,48,360]{2,1,0:T(8,128)(2,1)}), bf16[16,48,360]{2,1,0:T(8,128)(2,1)S(1)}, u32[]{:S(2)}, u32[]{:S(2)}) async-start(bf16[16,48,360]{2,1,0:T(8,128)(2,1)} %copy.95), calls=%async_computation.1 | async-start | bytes 1179648 | tf_op jit(solution)/shard_map/all_to_all | solution.py:201
Sparse Core Ops, SparseCore 0:
  10.6 93.6 all-gather.7
  106.9 90.0 all-gather.9
  222.0 63.0 reduce-scatter.9
  461.3 64.5 reduce-scatter.7
where the time goes:
time: 572 us; the launch traced here: 570 us
  blocking collectives  292 us (51%)
  waiting for transfers between devices  141 us (25%)
  local copies, waits for them, and re-layouts  70.9 us (12%)
  matrix products  37.3 us (7%)
  between operations  14.2 us (2%)
  starting transfers between devices  9.14 us (2%)
    unnamed x6, waiting for transfers between devices  125 us
    all_to_all x1, blocking collectives, shards(): lax.all_to_all(outgoing, 'expert', split_axis=0, concat_axis=0, tiled=True)  100 us
    unnamed x47, local copies, waits for them, and re-layouts  53.2 us
    all_gather x1, blocking collectives, shards(): lax.all_gather(key_weight, 'expert', axis=0, tiled=True)  40.1 us
    all_gather x1, blocking collectives, shards(): lax.all_gather(value_fresh, 'expert', axis=0, tiled=True)  35.5 us
    all_gather x1, blocking collectives, shards(): lax.all_gather(value_weight, 'expert', axis=0, tiled=True)  33.1 us
    all_gather x1, blocking collectives, shards(): lax.all_gather(key_rotary, 'expert', axis=0, tiled=True)  31.8 us
    all_gather x1, blocking collectives, shards(): moe_whole = lax.all_gather(first_out, 'mp', axis=1, tiled=True)  26.1 us
  transfers between devices with their start and end apart: 5, of which 3 were waited for; matrix products, arithmetic and copies ran while one was open for 8% of the time, Pallas kernels for 0%

commit v1 on v0

--- a/solution.py
+++ b/solution.py
@@ -72,7 +72,10 @@
     kv_cols = key_weight.shape[1]
     weight_parts = (
         lax.all_gather(w_query, "expert", axis=0, tiled=True),
-        lax.all_gather(key_weight, "expert", axis=0, tiled=True),
+        jnp.concatenate(
+            lax.all_to_all(jnp.stack([key_weight] * lax.axis_size("expert")), "expert", 0, 0),
+            axis=0,
+        ),
         lax.all_gather(value_weight, "expert", axis=0, tiled=True),
     )
     query_raw, key_raw, value_raw = tuple(

time: 572 us -> 545 us (0.953)
  blocking collectives: 292 us -> 253 us
  starting transfers between devices: 9.14 us -> 21 us
    all_gather x1 -> x0, blocking collectives: 40.1 us -> none  [shards(): lax.all_gather(key_weight, 'expert', axis=0, tiled=True)]
    all_to_all x0 -> x1, starting transfers between devices: none -> 11.8 us  [shards(): lax.all_to_all(jnp.stack([key_weight] * lax.axis_size('expert')), 'expert...]
    unnamed x6, waiting for transfers between devices: 125 us -> 113 us
    all_gather x1, waiting for transfers between devices: 0.02 us -> 7.13 us  [shards(): lax.all_gather(w_out, 'expert', axis=1, tiled=True)]
    unnamed x47 -> x44, local copies, waits for them, and re-layouts: 53.2 us -> 52 us
  transfers between devices with their start and end apart: 5 -> 6, of which waited for: 3 -> 4; matrix products, arithmetic and copies ran while one was open for 8% -> 9% of each run, Pallas kernels for 0% -> 0%
where the time goes in v1:
time: 545 us; the launch traced here: 543 us
  blocking collectives  253 us (46%)
  waiting for transfers between devices  137 us (25%)
  local copies, waits for them, and re-layouts  72.5 us (13%)
  matrix products  38 us (7%)
  starting transfers between devices  21 us (4%)
  between operations  14.2 us (3%)
  other arithmetic  7.02 us (1%)
    unnamed x6, waiting for transfers between devices  113 us
    all_to_all x1, blocking collectives, shards(): lax.all_to_all(outgoing, 'expert', split_axis=0, concat_axis=0, tiled=True)  100 us
    unnamed x44, local copies, waits for them, and re-layouts  52 us
    all_gather x1, blocking collectives, shards(): lax.all_gather(value_weight, 'expert', axis=0, tiled=True)  37 us
    all_gather x1, blocking collectives, shards(): lax.all_gather(value_fresh, 'expert', axis=0, tiled=True)  33.2 us
    all_gather x1, blocking collectives, shards(): lax.all_gather(key_rotary, 'expert', axis=0, tiled=True)  31.2 us
    all_gather x1, blocking collectives, shards(): moe_whole = lax.all_gather(first_out, 'mp', axis=1, tiled=True)  26.1 us
    all_gather x1, blocking collectives, shards(): whole_rows = lax.all_gather(local_rows, 'mp', axis=1, tiled=True)  25.4 us
  transfers between devices with their start and end apart: 6, of which 4 were waited for; matrix products, arithmetic and copies ran while one was open for 9% of the time, Pallas kernels for 0%

profile of v1, /device:TPU:1, one launch (start us, length us, event | category | flops | bytes accessed | tf_op | source)
XLA Modules:
  0.0 542.7 jit_solution(5569524478276868250)
XLA Ops:
  9.5 11.8 %all-to-all-start = ((bf16[16,180,64]{1,2,0:T(8,128)(2,1)}), bf16[16,180,64]{1,2,0:T(8,128)(2,1)}, u32[]{:S(2)}, u32[]{:S(2)}) async-start(bf16[16,180,64]{1,2,0:T(8,128)(2,1)} %stack.2), calls=%async_computation | async-start | bytes 1048576 | tf_op jit(solution)/shard_map/all_to_all | solution.py:76
  23.4 25.4 %all-gather = bf16[1,128,2880]{1,2,0:T(8,128)(2,1)S(1)} all-gather(bf16[1,128,360]{1,2,0:T(8,128)(2,1)} %param.17), channel_id=2, replica_groups=mesh['expert'=16,'mp'=8,'batch'=2] {'mp'}, dimensions={2}, use_global_device_ids=true | all-gather | bytes 829440 | tf_op jit(solution)/shard_map/all_gather | solution.py:69
  49.7 37.0 %all-gather.2 = bf16[16,180,64]{1,2,0:T(8,128)(2,1)S(1)} all-gather(bf16[1,180,64]{1,2,0:T(8,128)(2,1)S(1)} %bitcast.210), channel_id=1, replica_groups=mesh['expert'=16,'mp'=8,'batch'=2] {'expert'}, dimensions={0}, use_global_device_ids=true | all-gather | bytes 391680 | tf_op jit(solution)/shard_map/all_gather | solution.py:79
  91.5 33.2 %all_gather.25 = bf16[2048,64]{0,1:T(8,128)(2,1)} all-gather(bf16[128,64]{0,1:T(8,128)(2,1)S(1)} %convolution_convert_fusion.2), channel_id=1, replica_groups=mesh['expert'=16,'mp'=8,'batch'=2] {'expert'}, dimensions={0}, use_global_device_ids=true | all-gather | bytes 278528 | tf_op jit(solution)/shard_map/all_gather | solution.py:102
  131.7 31.2 %all_gather.22 = bf16[2048,64]{0,1:T(8,128)(2,1)S(1)} all-gather(bf16[128,64]{0,1:T(8,128)(2,1)S(1)} %pad_maximum_fusion), channel_id=1, replica_groups=mesh['expert'=16,'mp'=8,'batch'=2] {'expert'}, dimensions={0}, use_global_device_ids=true | all-gather | bytes 278528 | tf_op jit(solution)/shard_map/all_gather | solution.py:101
  163.9 4.4 reshape.402
  168.3 3.5 fusion.80
  172.7 7.0 %while.30 = (s32[]{:T(128)}, f32[1,1024]{1,0:T(1,128)S(1)}, s32[2048]{0:T(1024)S(1)}, bf16[1,2048,64]{2,1,0:T(8,128)(2,1)}, bf16[1,1024,64]{2,1,0:T(8,128)(2,1)}...) while((s32[]{:T(128)}, f32[1,1024]{1,0:T(1,128)S(1)}, ...), condition=%wide.region_3.4_spmd.clone, body=%wide.region_1.3_spmd.clone.sunk | while | flops 70255112 | bytes 437415 | solution.py:137
  179.7 12.6 %while.31 = (s32[]{:T(128)}, f32[1,1024,64]{1,2,0:T(8,128)S(1)}, f32[1,1024]{1,0:T(1,128)S(1)}, s32[2048]{0:T(1024)S(1)}, bf16[1,2048,64]{2,1,0:T(8,128)(2,1)}, ...) while((s32[]{:T(128)}, f32[1,1024,64]{1,2,0:T(8,128)S(1)}, ...), condition=%wide.region_6.7_spmd.clone, body=%wide.region_4.6_spmd.clone.sunk | while | flops 139068928 | bytes 3128526 | solution.py:153
  192.5 7.1 %all-gather.9.cloned.1.call-done = bf16[16,180,512]{2,1,0:T(8,128)(2,1)} async-done(((bf16[1,180,512]{2,1,0:T(8,128)(2,1)}), bf16[16,180,512]{2,1,0:T(8,128)(2,1)}) %all-gather.9.cloned.1.call-update) | async-done | bytes 2949136 | tf_op jit(solution)/shard_map/all_gather | solution.py:163
  199.6 4.4 reshape.406
  204.0 3.7 convolution_convert_fusion.1
  212.5 46.4 %reduce-scatter.10.cloned.1.call-done = bf16[128,360]{0,1:T(8,128)(2,1)} async-done(((bf16[128,2880]{0,1:T(8,128)(2,1)}), bf16[128,360]{0,1:T(8,128)(2,1)}) %reduce-scatter.10.cloned.1.call-update) | async-done | bytes 92176
  260.1 26.1 %all_gather.27 = bf16[128,2880]{0,1:T(8,128)(2,1)} all-gather(bf16[128,360]{0,1:T(8,128)(2,1)S(1)} %copy.83), channel_id=1, replica_groups=mesh['expert'=16,'mp'=8,'batch'=2] {'mp'}, dimensions={1}, use_global_device_ids=true | all-gather | bytes 829440 | tf_op jit(solution)/shard_map/all_gather | solution.py:185
  288.2 4.8 gather_fusion
  293.0 100.0 %all_to_all.15 = bf16[16,48,2880]{2,1,0:T(8,128)(2,1)S(1)} all-to-all(bf16[16,48,2880]{2,1,0:T(8,128)(2,1)} %bitcast.188), channel_id=1, replica_groups=mesh['expert'=16,'mp'=8,'batch'=2] {'expert'}, dimensions={0} | all-to-all | bytes 8847360 | tf_op jit(solution)/shard_map/all_to_all | solution.py:191
  393.0 3.5 fusion.38
  399.0 4.1 convolution_convert_fusion
  403.1 14.6 %copy.93 = bf16[16,48,2880]{1,0,2:T(8,128)(2,1)} copy(bf16[16,48,2880]{2,1,0:T(8,128)(2,1)} %convolution_convert_fusion) | data formatting | bytes 8847360
  417.7 17.1 %reshape.413 = bf16[2880,768]{1,0:T(8,128)(2,1)} reshape(bf16[2880,16,48]{2,1,0:T(8,128)(2,1)} %bitcast.186) | data formatting | bytes 8847360
  434.8 65.3 %reduce-scatter.8.cloned.1.call-done = bf16[360,768]{1,0:T(8,128)(2,1)} async-done(((bf16[2880,768]{1,0:T(8,128)(2,1)}), bf16[360,768]{1,0:T(8,128)(2,1)}) %reduce-scatter.8.cloned.1.call-update) | async-done | bytes 552976
  500.1 3.6 reshape.414
  506.3 9.0 %all-to-all-start.2 = ((bf16[16,48,360]{2,1,0:T(8,128)(2,1)}), bf16[16,48,360]{2,1,0:T(8,128)(2,1)S(1)}, u32[]{:S(2)}, u32[]{:S(2)}) async-start(bf16[16,48,360]{2,1,0:T(8,128)(2,1)} %copy.94), calls=%async_computation.2 | async-start | bytes 1179648 | tf_op jit(solution)/shard_map/all_to_all | solution.py:204
  516.1 16.6 %all-to-all-done.2 = bf16[16,48,360]{2,1,0:T(8,128)(2,1)S(1)} async-done(((bf16[16,48,360]{2,1,0:T(8,128)(2,1)}), bf16[16,48,360]{2,1,0:T(8,128)(2,1)S(1)}, u32[]{:S(2)}, u32[]{:S(2)}) %all-to-all-start.2) | async-done | bytes 552992 | tf_op jit(solution)/shard_map/all_to_all | solution.py:204
  (150 shorter events, 55.4 us)
Async XLA Ops:
  7.2 391.8 %copy-start = (bf16[1,360,2880]{2,1,0:T(8,128)(2,1)S(1)}, bf16[1,360,2880]{2,1,0:T(8,128)(2,1)}, u32[]{:S(2)}) copy-start(bf16[1,360,2880]{2,1,0:T(8,128)(2,1)} %param.27) | copy-start | bytes 6220804
  7.2 42.5 %copy-start.10 = (f32[8]{0:T(128)S(1)}, f32[8]{0:T(128)}, u32[]{:S(2)}) copy-start(f32[8]{0:T(128)} %param.24) | copy-start | bytes 100
  7.2 42.5 %copy-start.5 = (bf16[180,64]{0,1:T(8,128)(2,1)S(1)}, bf16[180,64]{0,1:T(8,128)(2,1)}, u32[]{:S(2)}) copy-start(bf16[180,64]{0,1:T(8,128)(2,1)} %param.22) | copy-start | bytes 69124
  7.2 156.7 %all-gather.7.cloned.1.call-start = ((), (), s32[]{:S(2)}) async-start(), calls=%async_computation.5 | async-start | bytes 3203072 | tf_op jit(solution)/shard_map/all_gather | solution.py:74
  9.5 116.1 %all-to-all-start = ((bf16[16,180,64]{1,2,0:T(8,128)(2,1)}), bf16[16,180,64]{1,2,0:T(8,128)(2,1)}, u32[]{:S(2)}, u32[]{:S(2)}) async-start(bf16[16,180,64]{1,2,0:T(8,128)(2,1)} %stack.2), calls=%async_computation | async-start | bytes 1048576 | tf_op jit(solution)/shard_map/all_to_all | solution.py:76
  21.3 178.3 %all-gather.9.cloned.1.call-start = ((), (), s32[]{:S(2)}) async-start(), calls=%async_computation.6 | async-start | bytes 3203072 | tf_op jit(solution)/shard_map/all_gather | solution.py:163
  22.1 67.5 %copy-start.2 = (s32[1,2048]{1,0:T(1,128)S(1)}, s32[1,2048]{1,0:T(1,128)}, u32[]{:S(2)}) copy-start(s32[1,2048]{1,0:T(1,128)} %param.18) | copy-start | bytes 24580
  22.1 236.8 %reduce-scatter.10.cloned.1.call-start = ((), (), s32[]{:S(2)}) async-start(), calls=%async_computation.8 | async-start | bytes 829440
  49.7 39.9 %copy-start.3 = (f32[8,128]{1,0:T(8,128)}, f32[8,128]{1,0:T(8,128)S(1)}, u32[]{:S(2)}) copy-start(f32[8,128]{1,0:T(8,128)S(1)} %broadcast_in_dim.74) | copy-start | bytes 12292
  90.9 0.6 copy-start.6
  163.9 4.4 copy-start.11
  163.9 4.4 copy-start.12
  179.7 12.7 %copy-start.4 = (f32[8,128]{1,0:T(8,128)S(1)}, f32[8,128]{1,0:T(8,128)}, u32[]{:S(2)}) copy-start(f32[8,128]{1,0:T(8,128)} %copy-done.3) | copy-start | bytes 12292
  204.0 3.8 copy-start.1
  204.0 3.9 copy-start.8
  207.7 292.4 %reduce-scatter.8.cloned.1.call-start = ((), (), s32[]{:S(2)}) async-start(), calls=%async_computation.7 | async-start | bytes 4976640
  208.1 79.8 %copy-start.7 = (f32[2880]{0:T(1024)S(1)}, f32[2880]{0:T(1024)}, u32[]{:S(2)}) copy-start(f32[2880]{0:T(1024)} %param.25) | copy-start | bytes 34564
  293.0 103.5 %slice-start = ((s8[4239360]{0:T(1024)(128)(4,1)}), s8[4194304]{0:T(1024)(128)(4,1)S(1)}, s32[]{:S(2)}) async-start(s8[4239360]{0:T(1024)(128)(4,1)} %bitcast.217), calls=%async_computation.9 | async-start | bytes 8388608
  393.0 3.6 slice-start.1
  503.7 11.6 %copy-start.9 = (f32[1,128,4]{1,2,0:T(4,128)S(1)}, f32[1,128,4]{1,2,0:T(4,128)}, u32[]{:S(2)}) copy-start(f32[1,128,4]{1,2,0:T(4,128)} %param.29) | copy-start | bytes 6148
  506.3 26.4 %all-to-all-start.2 = ((bf16[16,48,360]{2,1,0:T(8,128)(2,1)}), bf16[16,48,360]{2,1,0:T(8,128)(2,1)S(1)}, u32[]{:S(2)}, u32[]{:S(2)}) async-start(bf16[16,48,360]{2,1,0:T(8,128)(2,1)} %copy.94), calls=%async_computation.2 | async-start | bytes 1179648 | tf_op jit(solution)/shard_map/all_to_all | solution.py:204
Sparse Core Ops, SparseCore 0:
  10.6 97.1 all-gather.6
  110.4 89.1 all-gather.8
  207.8 51.0 reduce-scatter.9
  434.9 65.1 reduce-scatter.7
